TPU v7x, 256 devices: a whole 4x4x8 slice. The times are simulated.
256 devices in a mesh: dp: 4 (over x), ctx: 64 (over z, y, core).
Axes of the slice: x: 4, y: 4, z: 8, core: 2. Of those that a mesh axis runs over, the one named last changes fastest.
Arguments:
- inputs: bfloat16 [4, 16384, 2304], P('dp', 'ctx'), may hold values from -16 to 16
- query: bfloat16 [4, 16384, 1024], P('dp', 'ctx'), may hold values from -110 to 110
- w_key: bfloat16 [2304, 512], P('dp'), may hold values from -0.125 to 0.125
- w_value: bfloat16 [2304, 512], P('dp'), may hold values from -0.125 to 0.125
- doc_lengths: int32 [4, 16], P('dp'), may hold values from 1 to 4096, 16384 in all within a row
- grad_out: bfloat16 [4, 16384, 1024], P('dp', 'ctx'), may hold values from -6 to 6
Outputs:
- attended: bfloat16 [4, 16384, 1024], P('dp', 'ctx')
- grad_query: bfloat16 [4, 16384, 1024], P('dp', 'ctx')
- grad_input: bfloat16 [4, 16384, 2304], P('dp', 'ctx')
- grad_wkey: bfloat16 [2304, 512], P('dp')
- grad_wvalue: bfloat16 [2304, 512], P('dp')
All inputs are finite; a program needn't handle non-finite values.
Results may differ from a plain program's by a relative error of at most 0.025.
The roundings to bfloat16 on the way count: a program that leaves them out, or rounds other values in their place, can miss the bound.
Values may be sent and summed in bfloat16 or wider, within the bound.
No kernel may reach another device: no remote copies, remote signals or barrier semaphores. Data moves between devices by JAX's collectives and lax.ppermute only.
A program may use at most 128 MiB of HBM per device.

v0:
```python
import jax
import jax.numpy as jnp
from jax import lax
from jax.sharding import PartitionSpec as P

D = 2304
HQ = 4
HK = 2
HD = 256
WINDOW = 2048


FLOOR = -1e30


def from_behind(value, axis, by):
    peers = lax.axis_size(axis)
    pairs = [(i, i + by) for i in range(peers) if 0 <= i + by < peers]
    return lax.ppermute(value, axis, pairs)


def segment_of(lengths, positions):
    doc_ends = jnp.cumsum(lengths, dtype=jnp.int32)
    return jnp.sum(
        (doc_ends[None, :] <= positions[:, None]).astype(jnp.int32), axis=1, dtype=jnp.int32
    )


def band_mask(query_pos, query_seg, key_pos, key_seg):
    distance_gap = query_pos[:, None] - key_pos[None, :]
    inside = (distance_gap >= 0) & (distance_gap < WINDOW) & (key_pos[None, :] >= 0)
    return inside & (query_seg[:, None] == key_seg[None, :])


def masked_scores(query_heads, key_rows, allowed):
    key_heads = key_rows.reshape(key_rows.shape[0], HK, HD)
    scores = jnp.einsum(
        "qkgd,tkd->kgqt", query_heads, key_heads, preferred_element_type=jnp.float32
    ) * HD ** (-0.5)
    return jnp.where(allowed[None, None], scores, -jnp.inf)


def score_stats(scores):
    highest = jnp.maximum(jnp.max(scores, axis=-1), FLOOR)
    summed = jnp.sum(jnp.exp(scores - highest[..., None]), axis=-1)
    return (highest, summed)


def softmax_of(scores, log_total):
    softmax = jnp.exp(scores - log_total[..., None])
    return (softmax, softmax.astype(jnp.bfloat16))


def values_of(soft_half, value_rows):
    value_heads = value_rows.reshape(value_rows.shape[0], HK, HD)
    return jnp.einsum("kgqt,tkd->qkgd", soft_half, value_heads, preferred_element_type=jnp.float32)


def row_delta(upstream_heads, mixed_half):
    products = upstream_heads.astype(jnp.float32) * mixed_half.astype(jnp.float32)
    return jnp.transpose(jnp.sum(products, axis=-1), (1, 2, 0))


def band_grads(softmax, soft_half, query_heads, upstream_heads, delta_sum, key_rows, value_rows):
    span_rows = key_rows.shape[0]
    key_heads = key_rows.reshape(span_rows, HK, HD)
    value_heads = value_rows.reshape(span_rows, HK, HD)
    prob_grad = jnp.einsum(
        "qkgd,tkd->kgqt", upstream_heads, value_heads, preferred_element_type=jnp.float32
    )
    score_grad = (softmax * (prob_grad - delta_sum[..., None]) * HD ** (-0.5)).astype(jnp.bfloat16)
    query_grad = jnp.einsum(
        "kgqt,tkd->qkgd", score_grad, key_heads, preferred_element_type=jnp.float32
    )
    key_grad = jnp.einsum(
        "kgqt,qkgd->tkd", score_grad, query_heads, preferred_element_type=jnp.float32
    )
    value_grad = jnp.einsum(
        "kgqt,qkgd->tkd", soft_half, upstream_heads, preferred_element_type=jnp.float32
    )
    kv_grad = jnp.concatenate(
        [key_grad.reshape(span_rows, HK * HD), value_grad.reshape(span_rows, HK * HD)], axis=1
    )
    return (query_grad, kv_grad)


def shards(inputs, query, w_key, w_value, doc_lengths, grad_out):
    tokens = inputs[0]
    queries = query[0]
    upstream = grad_out[0]
    lengths = doc_lengths[0]
    tok_rows = tokens.shape[0]
    distant = WINDOW // tok_rows
    per_group = HQ // HK
    kv_width = HK * HD
    key_full, value_full = (
        lax.all_gather(w_key, "dp", axis=0, tiled=True),
        lax.all_gather(w_value, "dp", axis=0, tiled=True),
    )
    key_own = jnp.dot(tokens, key_full, preferred_element_type=jnp.float32).astype(jnp.bfloat16)
    value_own = jnp.dot(tokens, value_full, preferred_element_type=jnp.float32).astype(jnp.bfloat16)
    kv_own = jnp.concatenate([key_own, value_own], axis=1)
    earlier = jnp.concatenate(
        [from_behind(kv_own, "ctx", distance) for distance in range(distant, 0, -1)], axis=0
    )
    window = jnp.concatenate([earlier, kv_own], axis=0)
    device_index = lax.axis_index("ctx")
    first_row = device_index * tok_rows
    query_pos = first_row + jnp.arange(tok_rows, dtype=jnp.int32)
    key_pos = first_row - distant * tok_rows + jnp.arange((distant + 1) * tok_rows, dtype=jnp.int32)
    allowed = band_mask(
        query_pos, segment_of(lengths, query_pos), key_pos, segment_of(lengths, key_pos)
    )
    query_heads = queries.reshape(tok_rows, HK, per_group, HD)
    upstream_heads = upstream.reshape(tok_rows, HK, per_group, HD)
    scores = masked_scores(query_heads, window[:, :kv_width], allowed)
    highest, summed = score_stats(scores)
    log_total = highest + jnp.log(summed)
    softmax, soft_half = softmax_of(scores, log_total)
    mixed_half = values_of(soft_half, window[:, kv_width:]).astype(jnp.bfloat16)
    delta_sum = row_delta(upstream_heads, mixed_half)
    query_grad, window_grad = band_grads(
        softmax,
        soft_half,
        query_heads,
        upstream_heads,
        delta_sum,
        window[:, :kv_width],
        window[:, kv_width:],
    )
    own_grad = window_grad[distant * tok_rows :]
    earlier_grad = window_grad[: distant * tok_rows]
    for distance in range(1, distant + 1):
        lower = (distant - distance) * tok_rows
        own_grad = own_grad + from_behind(earlier_grad[lower : lower + tok_rows], "ctx", -distance)
    kv_grad = own_grad.astype(jnp.bfloat16)
    grad_input = (
        jnp.dot(kv_grad[:, :kv_width], key_full.T, preferred_element_type=jnp.float32)
        + jnp.dot(kv_grad[:, kv_width:], value_full.T, preferred_element_type=jnp.float32)
    ).astype(jnp.bfloat16)
    share_sum = lax.psum_scatter(
        lax.dot_general(
            tokens, kv_grad, (((0,), (0,)), ((), ())), preferred_element_type=jnp.float32
        ),
        "dp",
        scatter_dimension=0,
        tiled=True,
    )
    weight_grad = lax.psum(share_sum, "ctx").astype(jnp.bfloat16)
    attended = mixed_half.reshape(1, tok_rows, HQ * HD)
    grad_query = query_grad.astype(jnp.bfloat16).reshape(1, tok_rows, HQ * HD)
    return (
        attended,
        grad_query,
        grad_input.reshape(1, tok_rows, D),
        weight_grad[:, :kv_width],
        weight_grad[:, kv_width:],
    )


def solution(mesh):
    in_specs = (
        P("dp", "ctx", None),
        P("dp", "ctx", None),
        P("dp", None),
        P("dp", None),
        P("dp", None),
        P("dp", "ctx", None),
    )
    out_specs = (
        P("dp", "ctx", None),
        P("dp", "ctx", None),
        P("dp", "ctx", None),
        P("dp", None),
        P("dp", None),
    )
    return jax.shard_map(shards, mesh=mesh, in_specs=in_specs, out_specs=out_specs, check_vma=False)
```

profile of v0, /device:TPU:1, one launch (start us, length us, event | category | flops | bytes accessed | tf_op | source)
XLA Modules:
  0.0 777.9 jit_solution(336791386545529585)
XLA Ops:
  9.9 39.1 %all-gather.5.cloned.1.call-done = bf16[2304,512]{1,0:T(8,128)(2,1)} async-done(((bf16[576,512]{1,0:T(8,128)(2,1)}), bf16[2304,512]{1,0:T(8,128)(2,1)}) %all-gather.5.cloned.1.call-update) | async-done | bytes 2359312 | tf_op jit(solution)/shard_map/all_gather | solution.py:98
  48.9 2.4 convolution_convert_fusion.1
  51.4 35.0 %all-gather.3.cloned.1.call-done = bf16[2304,512]{1,0:T(8,128)(2,1)} async-done(((bf16[576,512]{1,0:T(8,128)(2,1)}), bf16[2304,512]{1,0:T(8,128)(2,1)}) %all-gather.3.cloned.1.call-update) | async-done | bytes 2359312 | tf_op jit(solution)/shard_map/all_gather | solution.py:97
  86.3 2.4 convolution_convert_fusion.2
  88.8 4.0 collective-permute-start
  92.8 4.2 collective-permute-start.1
  97.0 4.4 collective-permute-start.2
  101.4 3.0 collective-permute-start.3
  104.4 4.3 collective-permute-start.4
  108.8 3.3 fusion.8
  112.1 1.0 copy.67
  113.1 1.0 copy.100
  114.1 4.9 collective-permute-start.5
  119.0 1.1 constant_dynamic-update-slice_fusion.8
  120.1 2.5 collective-permute-start.6
  122.6 1.1 constant_dynamic-update-slice_fusion.7
  123.7 11.2 %collective-permute-done.2 = bf16[256,1024]{1,0:T(8,128)(2,1)} collective-permute-done((bf16[256,1024]{1,0:T(8,128)(2,1)S(1)}, bf16[256,1024]{1,0:T(8,128)(2,1)}, u32[]{:S(2)}, u32[]{:S(2)}) %collective-permute-start.2) | collective-permute-done | bytes 524320 | tf_op jit(solution)/shard_map/ppermute | solution.py:19
  134.8 2.1 collective-permute-start.7
  136.9 1.1 constant_dynamic-update-slice_fusion.6
  138.0 5.2 collective-permute-done.3
  143.2 1.1 constant_dynamic-update-slice_fusion.5
  144.3 1.1 constant_dynamic-update-slice_fusion.4
  145.5 5.4 collective-permute-done.7
  151.0 2.5 fusion.41
  153.5 5.0 reshape.159
  158.5 4.5 copy.84
  163.0 3.8 fusion.43
  166.9 1.3 exponential_reduce_fusion
  168.1 2.7 copy-done.1
  170.9 2.1 reshape.156
  173.0 5.3 fusion.15
  178.3 1.2 copy-done.2
  180.2 2.6 multiply_reduce_fusion
  182.8 2.6 fusion.2
  185.4 1.4 fusion.44
  187.6 0.9 fusion.31
  188.6 1.3 collective-permute-start.15
  189.9 1.3 collective-permute-start.14
  191.2 1.5 collective-permute-start.13
  192.7 1.3 collective-permute-start.12
  194.0 1.3 collective-permute-start.11
  195.3 35.3 %collective-permute-done.15 = f32[256,1024]{0,1:T(8,128)S(1)} collective-permute-done((f32[256,1024]{0,1:T(8,128)S(1)}, f32[256,1024]{0,1:T(8,128)S(1)}, u32[]{:S(2)}, u32[]{:S(2)}) %collective-permute-start.15) | collective-permute-done | bytes 1048608 | tf_op jit(solution)/shard_map/ppermute | solution.py:19
  230.5 1.3 collective-permute-start.10
  231.8 36.1 %collective-permute-done.14 = f32[256,1024]{0,1:T(8,128)S(1)} collective-permute-done((f32[256,1024]{0,1:T(8,128)S(1)}, f32[256,1024]{0,1:T(8,128)S(1)}, u32[]{:S(2)}, u32[]{:S(2)}) %collective-permute-start.14) | collective-permute-done | bytes 1048608 | tf_op jit(solution)/shard_map/ppermute | solution.py:19
  267.9 1.3 collective-permute-start.9
  269.2 12.6 %collective-permute-done.13 = f32[256,1024]{0,1:T(8,128)S(1)} collective-permute-done((f32[256,1024]{0,1:T(8,128)S(1)}, f32[256,1024]{0,1:T(8,128)S(1)}, u32[]{:S(2)}, u32[]{:S(2)}) %collective-permute-start.13) | collective-permute-done | bytes 1048608 | tf_op jit(solution)/shard_map/ppermute | solution.py:19
  281.8 1.9 collective-permute-start.8
  283.7 7.3 collective-permute-done.10
  291.0 41.2 %collective-permute-done.9 = f32[256,1024]{0,1:T(8,128)S(1)} collective-permute-done((f32[256,1024]{0,1:T(8,128)S(1)}, f32[256,1024]{0,1:T(8,128)S(1)}, u32[]{:S(2)}, u32[]{:S(2)}) %collective-permute-start.9) | collective-permute-done | bytes 1048608 | tf_op jit(solution)/shard_map/ppermute | solution.py:19
  332.2 7.7 collective-permute-done.8
  340.5 5.0 convolution_bitcast_fusion
  345.6 9.6 %copy.98 = f32[2304,1024]{1,0:T(8,128)} copy(f32[2304,1024]{0,1:T(8,128)} %convolution_bitcast_fusion) | data formatting | bytes 18874368
  355.2 1.0 copy-done.12
  356.3 1.0 copy.75
  357.3 4.4 convolution_convert_fusion
  361.7 1.0 copy.76
  362.7 2.6 fusion.38
  365.4 1.8 fusion.5
  367.2 124.1 %reduce-scatter.4.cloned.1.call-done = f32[576,1024]{1,0:T(8,128)} async-done(((f32[2304,1024]{1,0:T(8,128)}), f32[576,1024]{1,0:T(8,128)}) %reduce-scatter.4.cloned.1.call-update) | async-done | bytes 2359312
  491.3 3.2 copy.99
  494.5 272.8 %all-reduce.1 = bf16[576,1024]{0,1:T(8,128)(2,1)S(1)} all-reduce(f32[576,1024]{0,1:T(8,128)} %copy.99), channel_id=1, replica_groups=mesh['dp'=4,'ctx'=64] {'ctx'}, use_global_device_ids=true, to_apply=%region_7.8 | all-reduce | flops 589824 | bytes 3538944 | tf_op jit(solution)/shard_map/psum | solution.py:149
  767.2 1.0 fusion.42
  768.2 2.1 copy.77
  770.3 1.1 copy.78
  (52 shorter events, 5.0 us)
Async XLA Ops:
  7.2 41.8 %copy-start = (bf16[1,256,2304]{2,1,0:T(8,128)(2,1)S(1)}, bf16[1,256,2304]{2,1,0:T(8,128)(2,1)}, u32[]{:S(2)}) copy-start(bf16[1,256,2304]{2,1,0:T(8,128)(2,1)} %param.6) | copy-start | bytes 3538948
  7.2 41.7 %all-gather.5.cloned.1.call-start = ((), (), s32[]{:S(2)}) async-start(), calls=%async_computation.2 | async-start | bytes 2949120 | tf_op jit(solution)/shard_map/all_gather | solution.py:98
  7.9 78.4 %all-gather.3.cloned.1.call-start = ((), (), s32[]{:S(2)}) async-start(), calls=%async_computation.1 | async-start | bytes 2949120 | tf_op jit(solution)/shard_map/all_gather | solution.py:97
  8.7 482.6 %reduce-scatter.4.cloned.1.call-start = ((), (), s32[]{:S(2)}) async-start(), calls=%async_computation.3 | async-start | bytes 11796480
  9.8 102.2 %copy-start.10 = (bf16[1,256,1024]{2,1,0:T(8,128)(2,1)S(1)}, bf16[1,256,1024]{2,1,0:T(8,128)(2,1)}, u32[]{:S(2)}) copy-start(bf16[1,256,1024]{2,1,0:T(8,128)(2,1)} %param.11) | copy-start | bytes 1572868
  9.8 103.2 %copy-start.11 = (bf16[1,256,1024]{2,1,0:T(8,128)(2,1)S(1)}, bf16[1,256,1024]{2,1,0:T(8,128)(2,1)}, u32[]{:S(2)}) copy-start(bf16[1,256,1024]{2,1,0:T(8,128)(2,1)} %param.7) | copy-start | bytes 1572868
  88.8 25.2 %collective-permute-start = (bf16[256,1024]{1,0:T(8,128)(2,1)S(1)}, bf16[256,1024]{1,0:T(8,128)(2,1)}, u32[]{:S(2)}, u32[]{:S(2)}) collective-permute-start(bf16[256,1024]{1,0:T(8,128)(2,1)S(1)} %pad_maximum_fusion.1), channel_id=1, source_target_pairs={{0,8},{1,9},{2,10},{3,11},{4,12},{5,13},{6,14},{7,15},{8,16},{9,17... | collective-permute-start | bytes 1572872 | tf_op jit(solution)/shard_map/ppermute | solution.py:19
  92.8 27.2 %collective-permute-start.1 = (bf16[256,1024]{1,0:T(8,128)(2,1)S(1)}, bf16[256,1024]{1,0:T(8,128)(2,1)}, u32[]{:S(2)}, u32[]{:S(2)}) collective-permute-start(bf16[256,1024]{1,0:T(8,128)(2,1)S(1)} %pad_maximum_fusion.1), channel_id=1, source_target_pairs={{0,7},{1,8},{2,9},{3,10},{4,11},{5,12},{6,13},{7,14},{8,15},{9,16}... | collective-permute-start | bytes 1572872 | tf_op jit(solution)/shard_map/ppermute | solution.py:19
  97.0 37.8 %collective-permute-start.2 = (bf16[256,1024]{1,0:T(8,128)(2,1)S(1)}, bf16[256,1024]{1,0:T(8,128)(2,1)}, u32[]{:S(2)}, u32[]{:S(2)}) collective-permute-start(bf16[256,1024]{1,0:T(8,128)(2,1)S(1)} %pad_maximum_fusion.1), channel_id=1, source_target_pairs={{0,6},{1,7},{2,8},{3,9},{4,10},{5,11},{6,12},{7,13},{8,14},{9,15},... | collective-permute-start | bytes 1572872 | tf_op jit(solution)/shard_map/ppermute | solution.py:19
  101.4 41.8 %collective-permute-start.3 = (bf16[256,1024]{1,0:T(8,128)(2,1)S(1)}, bf16[256,1024]{1,0:T(8,128)(2,1)}, u32[]{:S(2)}, u32[]{:S(2)}) collective-permute-start(bf16[256,1024]{1,0:T(8,128)(2,1)S(1)} %pad_maximum_fusion.1), channel_id=1, source_target_pairs={{0,5},{1,6},{2,7},{3,8},{4,9},{5,10},{6,11},{7,12},{8,13},{9,14},{... | collective-permute-start | bytes 1572872 | tf_op jit(solution)/shard_map/ppermute | solution.py:19
  104.4 39.9 %collective-permute-start.4 = (bf16[256,1024]{1,0:T(8,128)(2,1)S(1)}, bf16[256,1024]{1,0:T(8,128)(2,1)}, u32[]{:S(2)}, u32[]{:S(2)}) collective-permute-start(bf16[256,1024]{1,0:T(8,128)(2,1)S(1)} %pad_maximum_fusion.1), channel_id=1, source_target_pairs={{0,4},{1,5},{2,6},{3,7},{4,8},{5,9},{6,10},{7,11},{8,12},{9,13},{1... | collective-permute-start | bytes 1572872 | tf_op jit(solution)/shard_map/ppermute | solution.py:19
  114.1 31.3 %collective-permute-start.5 = (bf16[256,1024]{1,0:T(8,128)(2,1)S(1)}, bf16[256,1024]{1,0:T(8,128)(2,1)S(1)}, u32[]{:S(2)}, u32[]{:S(2)}) collective-permute-start(bf16[256,1024]{1,0:T(8,128)(2,1)S(1)} %pad_maximum_fusion.1), channel_id=1, source_target_pairs={{0,3},{1,4},{2,5},{3,6},{4,7},{5,8},{6,9},{7,10},{8,11},{9,12},{10... | collective-permute-start | bytes 1572872 | tf_op jit(solution)/shard_map/ppermute | solution.py:19
  120.1 25.4 %collective-permute-start.6 = (bf16[256,1024]{1,0:T(8,128)(2,1)S(1)}, bf16[256,1024]{1,0:T(8,128)(2,1)S(1)}, u32[]{:S(2)}, u32[]{:S(2)}) collective-permute-start(bf16[256,1024]{1,0:T(8,128)(2,1)S(1)} %pad_maximum_fusion.1), channel_id=1, source_target_pairs={{0,2},{1,3},{2,4},{3,5},{4,6},{5,7},{6,8},{7,9},{8,10},{9,11},{10,... | collective-permute-start | bytes 1572872 | tf_op jit(solution)/shard_map/ppermute | solution.py:19
  134.8 16.1 %collective-permute-start.7 = (bf16[256,1024]{1,0:T(8,128)(2,1)S(1)}, bf16[256,1024]{1,0:T(8,128)(2,1)S(1)}, u32[]{:S(2)}, u32[]{:S(2)}) collective-permute-start(bf16[256,1024]{1,0:T(8,128)(2,1)S(1)} %pad_maximum_fusion.1), channel_id=1, source_target_pairs={{0,1},{1,2},{2,3},{3,4},{4,5},{5,6},{6,7},{7,8},{8,9},{9,10},{10,1... | collective-permute-start | bytes 1572872 | tf_op jit(solution)/shard_map/ppermute | solution.py:19
  166.8 4.0 copy-start.1
  166.9 4.0 copy-start.3
  173.0 6.5 copy-start.2
  173.0 7.2 copy-start.6
  173.0 7.2 copy-start.8
  180.2 2.6 copy-start.9
  182.8 2.6 copy-start.7
  185.4 2.2 copy-start.4
  188.6 42.0 %collective-permute-start.15 = (f32[256,1024]{0,1:T(8,128)S(1)}, f32[256,1024]{0,1:T(8,128)S(1)}, u32[]{:S(2)}, u32[]{:S(2)}) collective-permute-start(f32[256,1024]{0,1:T(8,128)S(1)} %get-tuple-element.31), channel_id=1, source_target_pairs={{8,0},{9,1},{10,2},{11,3},{12,4},{13,5},{14,6},{15,7},{16,8},{17,9... | collective-permute-start | bytes 3145736 | tf_op jit(solution)/shard_map/ppermute | solution.py:19
  189.9 78.1 %collective-permute-start.14 = (f32[256,1024]{0,1:T(8,128)S(1)}, f32[256,1024]{0,1:T(8,128)S(1)}, u32[]{:S(2)}, u32[]{:S(2)}) collective-permute-start(f32[256,1024]{0,1:T(8,128)S(1)} %get-tuple-element.32), channel_id=1, source_target_pairs={{7,0},{8,1},{9,2},{10,3},{11,4},{12,5},{13,6},{14,7},{15,8},{16,9}... | collective-permute-start | bytes 3145736 | tf_op jit(solution)/shard_map/ppermute | solution.py:19
  191.2 90.6 %collective-permute-start.13 = (f32[256,1024]{0,1:T(8,128)S(1)}, f32[256,1024]{0,1:T(8,128)S(1)}, u32[]{:S(2)}, u32[]{:S(2)}) collective-permute-start(f32[256,1024]{0,1:T(8,128)S(1)} %get-tuple-element.30), channel_id=1, source_target_pairs={{6,0},{7,1},{8,2},{9,3},{10,4},{11,5},{12,6},{13,7},{14,8},{15,9},... | collective-permute-start | bytes 3145736 | tf_op jit(solution)/shard_map/ppermute | solution.py:19
  192.7 91.0 %collective-permute-start.12 = (f32[256,1024]{0,1:T(8,128)S(1)}, f32[256,1024]{0,1:T(8,128)S(1)}, u32[]{:S(2)}, u32[]{:S(2)}) collective-permute-start(f32[256,1024]{0,1:T(8,128)S(1)} %get-tuple-element.29), channel_id=1, source_target_pairs={{5,0},{6,1},{7,2},{8,3},{9,4},{10,5},{11,6},{12,7},{13,8},{14,9},{... | collective-permute-start | bytes 3145736 | tf_op jit(solution)/shard_map/ppermute | solution.py:19
  194.0 89.7 %collective-permute-start.11 = (f32[256,1024]{0,1:T(8,128)S(1)}, f32[256,1024]{0,1:T(8,128)S(1)}, u32[]{:S(2)}, u32[]{:S(2)}) collective-permute-start(f32[256,1024]{0,1:T(8,128)S(1)} %get-tuple-element.28), channel_id=1, source_target_pairs={{4,0},{5,1},{6,2},{7,3},{8,4},{9,5},{10,6},{11,7},{12,8},{13,9},{1... | collective-permute-start | bytes 3145736 | tf_op jit(solution)/shard_map/ppermute | solution.py:19
  230.5 60.5 %collective-permute-start.10 = (f32[256,1024]{0,1:T(8,128)S(1)}, f32[256,1024]{0,1:T(8,128)S(1)}, u32[]{:S(2)}, u32[]{:S(2)}) collective-permute-start(f32[256,1024]{0,1:T(8,128)S(1)} %get-tuple-element.27), channel_id=1, source_target_pairs={{3,0},{4,1},{5,2},{6,3},{7,4},{8,5},{9,6},{10,7},{11,8},{12,9},{13... | collective-permute-start | bytes 3145736 | tf_op jit(solution)/shard_map/ppermute | solution.py:19
  267.9 64.3 %collective-permute-start.9 = (f32[256,1024]{0,1:T(8,128)S(1)}, f32[256,1024]{0,1:T(8,128)S(1)}, u32[]{:S(2)}, u32[]{:S(2)}) collective-permute-start(f32[256,1024]{0,1:T(8,128)S(1)} %get-tuple-element.26), channel_id=1, source_target_pairs={{2,0},{3,1},{4,2},{5,3},{6,4},{7,5},{8,6},{9,7},{10,8},{11,9},{12,... | collective-permute-start | bytes 3145736 | tf_op jit(solution)/shard_map/ppermute | solution.py:19
  281.8 58.1 %collective-permute-start.8 = (f32[256,1024]{0,1:T(8,128)S(1)}, f32[256,1024]{0,1:T(8,128)S(1)}, u32[]{:S(2)}, u32[]{:S(2)}) collective-permute-start(f32[256,1024]{0,1:T(8,128)S(1)} %get-tuple-element.25), channel_id=1, source_target_pairs={{1,0},{2,1},{3,2},{4,3},{5,4},{6,5},{7,6},{8,7},{9,8},{10,9},{11,1... | collective-permute-start | bytes 3145736 | tf_op jit(solution)/shard_map/ppermute | solution.py:19
  355.2 1.0 copy-start.12
  362.7 2.6 copy-start.5
Sparse Core Ops, SparseCore 0:
  9.8 39.0 all-gather.4
  50.7 35.5 all-gather.2
  355.4 135.8 reduce-scatter.3
where the time goes:
time: 782 us; the launch traced here: 778 us
  waiting for transfers between devices  361 us (46%)
  blocking collectives  273 us (35%)
  local copies, waits for them, and re-layouts  47.8 us (6%)
  starting transfers between devices  40.7 us (5%)
  matrix products  34.5 us (4%)
  between operations  14.2 us (2%)
    psum x1, blocking collectives, shards(): weight_grad = lax.psum(share_sum, 'ctx').astype(jnp.bfloat16)  273 us
    ppermute x16, waiting for transfers between devices, from_behind(): return lax.ppermute(value, axis, pairs)  162 us
    unnamed x4, waiting for transfers between devices  125 us
    ppermute x16, starting transfers between devices, from_behind(): return lax.ppermute(value, axis, pairs)  40.6 us
    all_gather x1, waiting for transfers between devices, shards(): lax.all_gather(w_value, 'dp', axis=0, tiled=True)  39.1 us
    all_gather x1, waiting for transfers between devices, shards(): lax.all_gather(w_key, 'dp', axis=0, tiled=True)  35 us
    unnamed x41, local copies, waits for them, and re-layouts  30.9 us
  transfers between devices with their start and end apart: 19, of which 12 were waited for; matrix products, arithmetic and copies ran while one was open for 3% of the time, Pallas kernels for 0%

commit v1 on v0

--- a/solution.py
+++ b/solution.py
@@ -132,21 +132,28 @@
     earlier_grad = window_grad[: distant * tok_rows]
     for distance in range(1, distant + 1):
         lower = (distant - distance) * tok_rows
-        own_grad = own_grad + from_behind(earlier_grad[lower : lower + tok_rows], "ctx", -distance)
+        own_grad = own_grad + from_behind(
+            earlier_grad[lower : lower + tok_rows].astype(jnp.bfloat16), "ctx", -distance
+        ).astype(jnp.float32)
     kv_grad = own_grad.astype(jnp.bfloat16)
     grad_input = (
         jnp.dot(kv_grad[:, :kv_width], key_full.T, preferred_element_type=jnp.float32)
         + jnp.dot(kv_grad[:, kv_width:], value_full.T, preferred_element_type=jnp.float32)
     ).astype(jnp.bfloat16)
-    share_sum = lax.psum_scatter(
-        lax.dot_general(
-            tokens, kv_grad, (((0,), (0,)), ((), ())), preferred_element_type=jnp.float32
-        ),
-        "dp",
-        scatter_dimension=0,
-        tiled=True,
-    )
-    weight_grad = lax.psum(share_sum, "ctx").astype(jnp.bfloat16)
+    dp_size = lax.axis_size("dp")
+    ctx_size = lax.axis_size("ctx")
+    row_share = D // dp_size
+    col_share = 2 * kv_width // ctx_size
+    weight_part = jnp.einsum(
+        "tar,tcj->acrj",
+        tokens.reshape(tok_rows, dp_size, row_share),
+        kv_grad.reshape(tok_rows, ctx_size, col_share),
+        preferred_element_type=jnp.float32,
+    ).reshape(dp_size * ctx_size, row_share, col_share)
+    share_sum = lax.psum_scatter(weight_part, ("dp", "ctx"), scatter_dimension=0, tiled=True)
+    share_sum = lax.optimization_barrier(share_sum)
+    gathered = lax.all_gather(share_sum.astype(jnp.bfloat16), "ctx", axis=0, tiled=True)
+    weight_grad = jnp.transpose(gathered, (1, 0, 2)).reshape(row_share, 2 * kv_width)
     attended = mixed_half.reshape(1, tok_rows, HQ * HD)
     grad_query = query_grad.astype(jnp.bfloat16).reshape(1, tok_rows, HQ * HD)
     return (

time: 782 us -> 1700 us (2.17)
  waiting for transfers between devices: 361 us -> 1550 us
  blocking collectives: 273 us -> 0 us
    reduce_scatter x0 -> x1, waiting for transfers between devices: none -> 1310 us  [shards(): lax.psum_scatter(weight_part, ('dp', 'ctx'), scatter_dimension=0, tiled=T...]
    psum x1 -> x0, blocking collectives: 273 us -> none  [shards(): weight_grad = lax.psum(share_sum, 'ctx').astype(jnp.bfloat16)]
    unnamed x4, waiting for transfers between devices: 125 us -> 1.41 us
    all_gather x0 -> x1, waiting for transfers between devices: none -> 66.8 us  [shards(): lax.all_gather(share_sum.astype(jnp.bfloat16), 'ctx', axis=0, tiled=True)]
    ppermute x16, waiting for transfers between devices: 162 us -> 97.8 us  [from_behind(): return lax.ppermute(value, axis, pairs)]
  transfers between devices with their start and end apart: 19 -> 20, of which waited for: 12 -> 11; matrix products, arithmetic and copies ran while one was open for 3% -> 1% of each run, Pallas kernels for 0% -> 0%
where the time goes in v1:
time: 1700 us
  waiting for transfers between devices  1550 us (91%)
  local copies, waits for them, and re-layouts  43.8 us (3%)
  starting transfers between devices  40.7 us (2%)
  matrix products  34.1 us (2%)
    reduce_scatter x1, waiting for transfers between devices, shards(): lax.psum_scatter(weight_part, ('dp', 'ctx'), scatter_dimension=0, tiled=T...  1310 us
    ppermute x16, waiting for transfers between devices, from_behind(): return lax.ppermute(value, axis, pairs)  97.8 us
    all_gather x1, waiting for transfers between devices, shards(): lax.all_gather(share_sum.astype(jnp.bfloat16), 'ctx', axis=0, tiled=True)  66.8 us
    ppermute x16, starting transfers between devices, from_behind(): return lax.ppermute(value, axis, pairs)  40.5 us
    all_gather x1, waiting for transfers between devices, shards(): lax.all_gather(w_value, 'dp', axis=0, tiled=True)  39.1 us
    all_gather x1, waiting for transfers between devices, shards(): lax.all_gather(w_key, 'dp', axis=0, tiled=True)  34.6 us
  transfers between devices with their start and end apart: 20, of which 11 were waited for; matrix products, arithmetic and copies ran while one was open for 1% of the time, Pallas kernels for 0%

profile of v1, /device:TPU:1, one launch (start us, length us, event | category | flops | bytes accessed | tf_op | source)
XLA Modules:
  0.0 1699.0 jit_solution(11646693558636724538)
XLA Ops:
  9.8 39.1 %all-gather.6.cloned.1.call-done = bf16[2304,512]{1,0:T(8,128)(2,1)} async-done(((bf16[576,512]{1,0:T(8,128)(2,1)}), bf16[2304,512]{1,0:T(8,128)(2,1)}) %all-gather.6.cloned.1.call-update) | async-done | bytes 2359312 | tf_op jit(solution)/shard_map/all_gather | solution.py:98
  48.9 2.8 convolution_convert_fusion.1
  51.7 34.6 %all-gather.4.cloned.1.call-done = bf16[2304,512]{1,0:T(8,128)(2,1)} async-done(((bf16[576,512]{1,0:T(8,128)(2,1)}), bf16[2304,512]{1,0:T(8,128)(2,1)}) %all-gather.4.cloned.1.call-update) | async-done | bytes 2359312 | tf_op jit(solution)/shard_map/all_gather | solution.py:97
  86.3 2.4 convolution_convert_fusion.2
  88.8 4.0 collective-permute-start
  92.8 4.2 collective-permute-start.1
  97.0 4.4 collective-permute-start.2
  101.4 3.0 collective-permute-start.3
  104.4 3.6 collective-permute-start.4
  108.0 3.3 fusion.9
  111.5 1.2 copy.104
  112.8 5.6 collective-permute-start.5
  118.5 1.1 constant_dynamic-update-slice_fusion.8
  119.5 2.5 collective-permute-start.6
  122.1 1.1 constant_dynamic-update-slice_fusion.7
  123.1 11.7 collective-permute-done.2
  134.8 2.1 collective-permute-start.7
  136.9 1.1 constant_dynamic-update-slice_fusion.6
  138.0 5.2 collective-permute-done.3
  143.2 1.1 constant_dynamic-update-slice_fusion.5
  144.5 6.4 collective-permute-done.7
  151.0 2.5 fusion.35
  153.5 5.0 reshape.168
  158.5 4.7 copy.89
  163.2 3.7 fusion.37
  166.9 1.2 exponential_reduce_fusion
  168.2 2.7 copy-done.2
  170.9 2.2 reshape.165
  173.1 5.3 fusion.16
  178.4 1.2 copy-done.3
  179.6 2.2 copy-done.7
  181.8 2.6 multiply_reduce_fusion
  184.4 4.0 fusion.3
  188.4 3.8 fusion.38
  192.2 2.9 fusion
  195.1 0.8 copy-done
  195.8 3.7 fusion.34
  199.6 1.3 collective-permute-start.15
  200.9 1.5 collective-permute-start.14
  202.4 1.3 collective-permute-start.13
  203.7 1.3 collective-permute-start.12
  205.0 1.3 collective-permute-start.11
  206.3 25.9 %collective-permute-done.15 = bf16[256,1024]{0,1:T(8,128)(2,1)S(1)} collective-permute-done((bf16[256,1024]{0,1:T(8,128)(2,1)S(1)}, bf16[256,1024]{0,1:T(8,128)(2,1)S(1)}, u32[]{:S(2)}, u32[]{:S(2)}) %collective-permute-start.15) | collective-permute-done | bytes 524320 | tf_op jit(solution)/shard_map/ppermute | solution.py:19
  232.2 1.3 collective-permute-start.10
  233.5 23.1 %collective-permute-done.14 = bf16[256,1024]{0,1:T(8,128)(2,1)S(1)} collective-permute-done((bf16[256,1024]{0,1:T(8,128)(2,1)S(1)}, bf16[256,1024]{0,1:T(8,128)(2,1)S(1)}, u32[]{:S(2)}, u32[]{:S(2)}) %collective-permute-start.14) | collective-permute-done | bytes 524320 | tf_op jit(solution)/shard_map/ppermute | solution.py:19
  256.6 1.3 collective-permute-start.9
  257.9 1.9 collective-permute-start.8
  259.8 1.6 copy.78
  261.4 24.5 %collective-permute-done.9 = bf16[256,1024]{0,1:T(8,128)(2,1)} collective-permute-done((bf16[256,1024]{0,1:T(8,128)(2,1)}, bf16[256,1024]{0,1:T(8,128)(2,1)}, u32[]{:S(2)}, u32[]{:S(2)}) %collective-permute-start.9) | collective-permute-done | bytes 524320 | tf_op jit(solution)/shard_map/ppermute | solution.py:19
  285.9 0.9 collective-permute-done.8
  286.9 2.6 fusion.30
  289.4 1.6 convolution_bitcast_fusion
  291.0 5.0 copy.79
  296.1 1314.6 %reduce-scatter.2.cloned.1.call-done = f32[1,576,16]{1,2,0:T(8,128)} async-done(((f32[256,576,16]{1,2,0:T(8,128)}), f32[1,576,16]{1,2,0:T(8,128)}) %reduce-scatter.2.cloned.1.call-update) | async-done | bytes 36880 | tf_op jit(solution)/shard_map/reduce_scatter | solution.py:153
  1610.7 1.4 convert_element_type.99
  1612.1 1.0 copy.80
  1613.1 3.7 convolution_convert_fusion
  1616.9 1.0 copy.81
  1617.9 2.5 fusion.31
  1620.4 1.9 fusion.6
  1622.2 66.8 %all-gather.8.cloned.1.call-done = bf16[64,576,16]{1,2,0:T(8,128)(2,1)} async-done(((bf16[1,576,16]{1,2,0:T(8,128)(2,1)}), bf16[64,576,16]{1,2,0:T(8,128)(2,1)}) %all-gather.8.cloned.1.call-update) | async-done | bytes 1179664 | tf_op jit(solution)/shard_map/all_gather | solution.py:155
  1689.0 1.4 fusion.36
  1690.4 1.1 copy.82
  1691.5 1.1 copy.83
  (58 shorter events, 3.2 us)
Async XLA Ops:
  7.2 79.2 %copy-start.10 = (bf16[1,256,2304]{2,1,0:T(8,128)(2,1)S(1)}, bf16[1,256,2304]{2,1,0:T(8,128)(2,1)}, u32[]{:S(2)}) copy-start(bf16[1,256,2304]{2,1,0:T(8,128)(2,1)} %param.6) | copy-start | bytes 3538948
  7.2 41.7 %all-gather.6.cloned.1.call-start = ((), (), s32[]{:S(2)}) async-start(), calls=%async_computation.2 | async-start | bytes 2949120 | tf_op jit(solution)/shard_map/all_gather | solution.py:98
  7.9 78.4 %all-gather.4.cloned.1.call-start = ((), (), s32[]{:S(2)}) async-start(), calls=%async_computation.1 | async-start | bytes 2949120 | tf_op jit(solution)/shard_map/all_gather | solution.py:97
  8.7 1602.0 %reduce-scatter.2.cloned.1.call-start = ((), (), s32[]{:S(2)}) async-start(), calls=%async_computation.3 | async-start | bytes 10526720 | tf_op jit(solution)/shard_map/reduce_scatter | solution.py:153
  9.8 101.5 %copy-start.12 = (bf16[1,256,1024]{2,1,0:T(8,128)(2,1)S(1)}, bf16[1,256,1024]{2,1,0:T(8,128)(2,1)}, u32[]{:S(2)}) copy-start(bf16[1,256,1024]{2,1,0:T(8,128)(2,1)} %param.11) | copy-start | bytes 1572868
  88.8 23.9 %collective-permute-start = (bf16[256,1024]{1,0:T(8,128)(2,1)S(1)}, bf16[256,1024]{1,0:T(8,128)(2,1)}, u32[]{:S(2)}, u32[]{:S(2)}) collective-permute-start(bf16[256,1024]{1,0:T(8,128)(2,1)S(1)} %pad_maximum_fusion.1), channel_id=1, source_target_pairs={{0,8},{1,9},{2,10},{3,11},{4,12},{5,13},{6,14},{7,15},{8,16},{9,17... | collective-permute-start | bytes 1572872 | tf_op jit(solution)/shard_map/ppermute | solution.py:19
  92.8 26.7 %collective-permute-start.1 = (bf16[256,1024]{1,0:T(8,128)(2,1)S(1)}, bf16[256,1024]{1,0:T(8,128)(2,1)}, u32[]{:S(2)}, u32[]{:S(2)}) collective-permute-start(bf16[256,1024]{1,0:T(8,128)(2,1)S(1)} %pad_maximum_fusion.1), channel_id=1, source_target_pairs={{0,7},{1,8},{2,9},{3,10},{4,11},{5,12},{6,13},{7,14},{8,15},{9,16}... | collective-permute-start | bytes 1572872 | tf_op jit(solution)/shard_map/ppermute | solution.py:19
  97.0 37.8 %collective-permute-start.2 = (bf16[256,1024]{1,0:T(8,128)(2,1)S(1)}, bf16[256,1024]{1,0:T(8,128)(2,1)}, u32[]{:S(2)}, u32[]{:S(2)}) collective-permute-start(bf16[256,1024]{1,0:T(8,128)(2,1)S(1)} %pad_maximum_fusion.1), channel_id=1, source_target_pairs={{0,6},{1,7},{2,8},{3,9},{4,10},{5,11},{6,12},{7,13},{8,14},{9,15},... | collective-permute-start | bytes 1572872 | tf_op jit(solution)/shard_map/ppermute | solution.py:19
  101.4 41.8 %collective-permute-start.3 = (bf16[256,1024]{1,0:T(8,128)(2,1)S(1)}, bf16[256,1024]{1,0:T(8,128)(2,1)}, u32[]{:S(2)}, u32[]{:S(2)}) collective-permute-start(bf16[256,1024]{1,0:T(8,128)(2,1)S(1)} %pad_maximum_fusion.1), channel_id=1, source_target_pairs={{0,5},{1,6},{2,7},{3,8},{4,9},{5,10},{6,11},{7,12},{8,13},{9,14},{... | collective-permute-start | bytes 1572872 | tf_op jit(solution)/shard_map/ppermute | solution.py:19
  104.4 39.9 %collective-permute-start.4 = (bf16[256,1024]{1,0:T(8,128)(2,1)S(1)}, bf16[256,1024]{1,0:T(8,128)(2,1)S(1)}, u32[]{:S(2)}, u32[]{:S(2)}) collective-permute-start(bf16[256,1024]{1,0:T(8,128)(2,1)S(1)} %pad_maximum_fusion.1), channel_id=1, source_target_pairs={{0,4},{1,5},{2,6},{3,7},{4,8},{5,9},{6,10},{7,11},{8,12},{9,13},{1... | collective-permute-start | bytes 1572872 | tf_op jit(solution)/shard_map/ppermute | solution.py:19
  112.8 50.5 %copy-start.8 = (bf16[1,256,1024]{1,2,0:T(8,128)(2,1)}, bf16[1,256,1024]{1,2,0:T(8,128)(2,1)S(1)}, u32[]{:S(2)}) copy-start(bf16[1,256,1024]{1,2,0:T(8,128)(2,1)S(1)} %copy.104) | copy-start | bytes 1572868
  112.8 31.5 %collective-permute-start.5 = (bf16[256,1024]{1,0:T(8,128)(2,1)S(1)}, bf16[256,1024]{1,0:T(8,128)(2,1)S(1)}, u32[]{:S(2)}, u32[]{:S(2)}) collective-permute-start(bf16[256,1024]{1,0:T(8,128)(2,1)S(1)} %pad_maximum_fusion.1), channel_id=1, source_target_pairs={{0,3},{1,4},{2,5},{3,6},{4,7},{5,8},{6,9},{7,10},{8,11},{9,12},{10... | collective-permute-start | bytes 1572872 | tf_op jit(solution)/shard_map/ppermute | solution.py:19
  119.5 24.9 %collective-permute-start.6 = (bf16[256,1024]{1,0:T(8,128)(2,1)S(1)}, bf16[256,1024]{1,0:T(8,128)(2,1)S(1)}, u32[]{:S(2)}, u32[]{:S(2)}) collective-permute-start(bf16[256,1024]{1,0:T(8,128)(2,1)S(1)} %pad_maximum_fusion.1), channel_id=1, source_target_pairs={{0,2},{1,3},{2,4},{3,5},{4,6},{5,7},{6,8},{7,9},{8,10},{9,11},{10,... | collective-permute-start | bytes 1572872 | tf_op jit(solution)/shard_map/ppermute | solution.py:19
  134.8 16.1 collective-permute-start.7
  166.9 4.0 copy-start.2
  166.9 4.0 copy-start.4
  173.1 6.5 copy-start.3
  173.1 8.7 copy-start.7
  178.4 13.8 copy-start.1
  184.4 4.0 copy-start.9
  192.1 3.7 copy-start
  199.6 32.6 %collective-permute-start.15 = (bf16[256,1024]{0,1:T(8,128)(2,1)S(1)}, bf16[256,1024]{0,1:T(8,128)(2,1)S(1)}, u32[]{:S(2)}, u32[]{:S(2)}) collective-permute-start(bf16[256,1024]{0,1:T(8,128)(2,1)S(1)} %get-tuple-element.26), channel_id=1, source_target_pairs={{8,0},{9,1},{10,2},{11,3},{12,4},{13,5},{14,6},{15,7},{16,8},{17,9... | collective-permute-start | bytes 1572872 | tf_op jit(solution)/shard_map/ppermute | solution.py:19
  200.9 55.7 %collective-permute-start.14 = (bf16[256,1024]{0,1:T(8,128)(2,1)S(1)}, bf16[256,1024]{0,1:T(8,128)(2,1)S(1)}, u32[]{:S(2)}, u32[]{:S(2)}) collective-permute-start(bf16[256,1024]{0,1:T(8,128)(2,1)S(1)} %get-tuple-element.27), channel_id=1, source_target_pairs={{7,0},{8,1},{9,2},{10,3},{11,4},{12,5},{13,6},{14,7},{15,8},{16,9}... | collective-permute-start | bytes 1572872 | tf_op jit(solution)/shard_map/ppermute | solution.py:19
  202.4 55.5 %collective-permute-start.13 = (bf16[256,1024]{0,1:T(8,128)(2,1)S(1)}, bf16[256,1024]{0,1:T(8,128)(2,1)S(1)}, u32[]{:S(2)}, u32[]{:S(2)}) collective-permute-start(bf16[256,1024]{0,1:T(8,128)(2,1)S(1)} %get-tuple-element.28), channel_id=1, source_target_pairs={{6,0},{7,1},{8,2},{9,3},{10,4},{11,5},{12,6},{13,7},{14,8},{15,9},... | collective-permute-start | bytes 1572872 | tf_op jit(solution)/shard_map/ppermute | solution.py:19
  203.7 57.7 %collective-permute-start.12 = (bf16[256,1024]{0,1:T(8,128)(2,1)}, bf16[256,1024]{0,1:T(8,128)(2,1)S(1)}, u32[]{:S(2)}, u32[]{:S(2)}) collective-permute-start(bf16[256,1024]{0,1:T(8,128)(2,1)} %get-tuple-element.29), channel_id=1, source_target_pairs={{5,0},{6,1},{7,2},{8,3},{9,4},{10,5},{11,6},{12,7},{13,8},{14,9},{... | collective-permute-start | bytes 1572872 | tf_op jit(solution)/shard_map/ppermute | solution.py:19
  205.0 56.4 %collective-permute-start.11 = (bf16[256,1024]{0,1:T(8,128)(2,1)}, bf16[256,1024]{0,1:T(8,128)(2,1)}, u32[]{:S(2)}, u32[]{:S(2)}) collective-permute-start(bf16[256,1024]{0,1:T(8,128)(2,1)} %get-tuple-element.30), channel_id=1, source_target_pairs={{4,0},{5,1},{6,2},{7,3},{8,4},{9,5},{10,6},{11,7},{12,8},{13,9},{1... | collective-permute-start | bytes 1572872 | tf_op jit(solution)/shard_map/ppermute | solution.py:19
  232.2 29.2 %collective-permute-start.10 = (bf16[256,1024]{0,1:T(8,128)(2,1)}, bf16[256,1024]{0,1:T(8,128)(2,1)}, u32[]{:S(2)}, u32[]{:S(2)}) collective-permute-start(bf16[256,1024]{0,1:T(8,128)(2,1)} %get-tuple-element.31), channel_id=1, source_target_pairs={{3,0},{4,1},{5,2},{6,3},{7,4},{8,5},{9,6},{10,7},{11,8},{12,9},{13... | collective-permute-start | bytes 1572872 | tf_op jit(solution)/shard_map/ppermute | solution.py:19
  256.6 29.4 %collective-permute-start.9 = (bf16[256,1024]{0,1:T(8,128)(2,1)}, bf16[256,1024]{0,1:T(8,128)(2,1)}, u32[]{:S(2)}, u32[]{:S(2)}) collective-permute-start(bf16[256,1024]{0,1:T(8,128)(2,1)} %get-tuple-element.32), channel_id=1, source_target_pairs={{2,0},{3,1},{4,2},{5,3},{6,4},{7,5},{8,6},{9,7},{10,8},{11,9},{12,... | collective-permute-start | bytes 1572872 | tf_op jit(solution)/shard_map/ppermute | solution.py:19
  257.9 29.0 %collective-permute-start.8 = (bf16[256,1024]{0,1:T(8,128)(2,1)}, bf16[256,1024]{0,1:T(8,128)(2,1)}, u32[]{:S(2)}, u32[]{:S(2)}) collective-permute-start(bf16[256,1024]{0,1:T(8,128)(2,1)} %get-tuple-element.25), channel_id=1, source_target_pairs={{1,0},{2,1},{3,2},{4,3},{5,4},{6,5},{7,6},{8,7},{9,8},{10,9},{11,1... | collective-permute-start | bytes 1572872 | tf_op jit(solution)/shard_map/ppermute | solution.py:19
  261.4 24.5 %copy-start.11 = (bf16[256,1024]{0,1:T(8,128)(2,1)}, bf16[256,1024]{0,1:T(8,128)(2,1)S(1)}, u32[]{:S(2)}) copy-start(bf16[256,1024]{0,1:T(8,128)(2,1)S(1)} %collective-permute-done.12) | copy-start | bytes 1572868
  296.0 1316.1 %copy-start.13 = (bf16[2,256,2,256]{3,1,2,0:T(8,128)(2,1)S(1)}, bf16[2,256,2,256]{3,1,2,0:T(8,128)(2,1)}, u32[]{:S(2)}) copy-start(bf16[2,256,2,256]{3,1,2,0:T(8,128)(2,1)} %get-tuple-element.40) | copy-start | bytes 1572868
  296.0 1317.1 %copy-start.6 = (bf16[2304,2,256,1]{0,2,3,1:T(8,128)(2,1)S(1)}, bf16[2304,2,256,1]{0,2,3,1:T(8,128)(2,1)}, u32[]{:S(2)}) copy-start(bf16[2304,2,256,1]{0,2,3,1:T(8,128)(2,1)} %copy.89) | copy-start | bytes 7077892
  296.0 1393.0 %all-gather.8.cloned.1.call-start = ((), (), s32[]{:S(2)}) async-start(), calls=%async_computation.4 | async-start | bytes 1331200 | tf_op jit(solution)/shard_map/all_gather | solution.py:155
  1616.8 3.5 copy-start.5
Sparse Core Ops, SparseCore 0:
  9.8 39.0 all-gather.5
  50.7 35.5 all-gather.3
  296.2 1314.4 reduce-scatter.1
  1613.8 75.1 all-gather.7

commit v2 on v1

--- a/solution.py
+++ b/solution.py
@@ -11,10 +11,15 @@
 
 
 FLOOR = -1e30
+CTX = ("z", "y", "c")
+
+
+def ctx_size():
+    return lax.axis_size("z") * lax.axis_size("y") * lax.axis_size("c")
 
 
 def from_behind(value, axis, by):
-    peers = lax.axis_size(axis)
+    peers = ctx_size()
     pairs = [(i, i + by) for i in range(peers) if 0 <= i + by < peers]
     return lax.ppermute(value, axis, pairs)
 
@@ -93,18 +98,18 @@
     distant = WINDOW // tok_rows
     per_group = HQ // HK
     kv_width = HK * HD
-    key_full, value_full = (
-        lax.all_gather(w_key, "dp", axis=0, tiled=True),
-        lax.all_gather(w_value, "dp", axis=0, tiled=True),
-    )
+    core = lax.axis_index("c")
+    mine = jnp.stack([w_key, w_value])[core]
+    both = lax.all_gather(lax.all_gather(mine, "dp", axis=0, tiled=True), "c", axis=0)
+    key_full, value_full = both[0], both[1]
     key_own = jnp.dot(tokens, key_full, preferred_element_type=jnp.float32).astype(jnp.bfloat16)
     value_own = jnp.dot(tokens, value_full, preferred_element_type=jnp.float32).astype(jnp.bfloat16)
     kv_own = jnp.concatenate([key_own, value_own], axis=1)
     earlier = jnp.concatenate(
-        [from_behind(kv_own, "ctx", distance) for distance in range(distant, 0, -1)], axis=0
+        [from_behind(kv_own, CTX, distance) for distance in range(distant, 0, -1)], axis=0
     )
     window = jnp.concatenate([earlier, kv_own], axis=0)
-    device_index = lax.axis_index("ctx")
+    device_index = lax.axis_index(CTX)
     first_row = device_index * tok_rows
     query_pos = first_row + jnp.arange(tok_rows, dtype=jnp.int32)
     key_pos = first_row - distant * tok_rows + jnp.arange((distant + 1) * tok_rows, dtype=jnp.int32)
@@ -133,7 +138,7 @@
     for distance in range(1, distant + 1):
         lower = (distant - distance) * tok_rows
         own_grad = own_grad + from_behind(
-            earlier_grad[lower : lower + tok_rows].astype(jnp.bfloat16), "ctx", -distance
+            earlier_grad[lower : lower + tok_rows].astype(jnp.bfloat16), CTX, -distance
         ).astype(jnp.float32)
     kv_grad = own_grad.astype(jnp.bfloat16)
     grad_input = (
@@ -141,19 +146,25 @@
         + jnp.dot(kv_grad[:, kv_width:], value_full.T, preferred_element_type=jnp.float32)
     ).astype(jnp.bfloat16)
     dp_size = lax.axis_size("dp")
-    ctx_size = lax.axis_size("ctx")
+    z_size, y_size, c_size = lax.axis_size("z"), lax.axis_size("y"), lax.axis_size("c")
     row_share = D // dp_size
-    col_share = 2 * kv_width // ctx_size
+    rows_z = row_share // z_size
+    cols_cy = 2 * kv_width // (c_size * y_size)
     weight_part = jnp.einsum(
-        "tar,tcj->acrj",
-        tokens.reshape(tok_rows, dp_size, row_share),
-        kv_grad.reshape(tok_rows, ctx_size, col_share),
+        "tazr,tcyj->cyazrj",
+        tokens.reshape(tok_rows, dp_size, z_size, rows_z),
+        kv_grad.reshape(tok_rows, c_size, y_size, cols_cy),
         preferred_element_type=jnp.float32,
-    ).reshape(dp_size * ctx_size, row_share, col_share)
-    share_sum = lax.psum_scatter(weight_part, ("dp", "ctx"), scatter_dimension=0, tiled=True)
-    share_sum = lax.optimization_barrier(share_sum)
-    gathered = lax.all_gather(share_sum.astype(jnp.bfloat16), "ctx", axis=0, tiled=True)
-    weight_grad = jnp.transpose(gathered, (1, 0, 2)).reshape(row_share, 2 * kv_width)
+    )
+    part = lax.psum_scatter(weight_part, "c", scatter_dimension=0, tiled=True)[0]
+    part = lax.psum_scatter(part, "y", scatter_dimension=0, tiled=True)[0]
+    part = lax.psum_scatter(part, "dp", scatter_dimension=0, tiled=True)[0]
+    part = lax.psum_scatter(part, "z", scatter_dimension=0, tiled=True)
+    part = lax.optimization_barrier(part).astype(jnp.bfloat16)
+    part = lax.all_gather(part, "z", axis=0, tiled=True).reshape(row_share, cols_cy)
+    part = lax.all_gather(part, "y", axis=0)
+    part = lax.all_gather(part, "c", axis=0)
+    weight_grad = jnp.transpose(part, (2, 0, 1, 3)).reshape(row_share, 2 * kv_width)
     attended = mixed_half.reshape(1, tok_rows, HQ * HD)
     grad_query = query_grad.astype(jnp.bfloat16).reshape(1, tok_rows, HQ * HD)
     return (
@@ -166,19 +177,11 @@
 
 
 def solution(mesh):
-    in_specs = (
-        P("dp", "ctx", None),
-        P("dp", "ctx", None),
-        P("dp", None),
-        P("dp", None),
-        P("dp", None),
-        P("dp", "ctx", None),
+    z_size = mesh.devices.shape[1] // 8
+    split = jax.sharding.Mesh(
+        mesh.devices.reshape(mesh.devices.shape[0], z_size, 4, 2), ("dp",) + CTX
     )
-    out_specs = (
-        P("dp", "ctx", None),
-        P("dp", "ctx", None),
-        P("dp", "ctx", None),
-        P("dp", None),
-        P("dp", None),
-    )
-    return jax.shard_map(shards, mesh=mesh, in_specs=in_specs, out_specs=out_specs, check_vma=False)
+    tokens_spec = P("dp", CTX, None)
+    in_specs = (tokens_spec, tokens_spec, P("dp", None), P("dp", None), P("dp", None), tokens_spec)
+    out_specs = (tokens_spec, tokens_spec, tokens_spec, P("dp", None), P("dp", None))
+    return jax.shard_map(shards, mesh=split, in_specs=in_specs, out_specs=out_specs, check_vma=False)

time: 1700 us -> 496 us (0.29)
  waiting for transfers between devices: 1550 us -> 347 us
  blocking collectives: 0 us -> 29.7 us
  local copies, waits for them, and re-layouts: 43.8 us -> 19 us
    reduce_scatter x1 -> x3, waiting for transfers between devices: 1310 us -> 134 us  [the longest x1 56.8 us: shards(): part = lax.psum_scatter(part, 'y', scatter_dimension=0, tiled=True)[0]]
    all_gather x3, waiting for transfers between devices: 140 us -> 78.4 us  [the longest x1 40 us: shards(): lax.all_gather(mine, 'dp', axis=0, tiled=True)]
    unnamed x4 -> x8, waiting for transfers between devices: 1.41 us -> 35.3 us
    all_gather x0 -> x2, blocking collectives: none -> 29.7 us  [the longest x1 18.2 us: shards(): lax.all_gather(part, 'z', axis=0, tiled=True).reshape(row_share, cols_cy)]
  transfers between devices with their start and end apart: 20 -> 23, of which waited for: 11 -> 14; matrix products, arithmetic and copies ran while one was open for 1% -> 4% of each run, Pallas kernels for 0% -> 0%
where the time goes in v2:
time: 496 us; the launch traced here: 495 us
  waiting for transfers between devices  347 us (70%)
  starting transfers between devices  39.9 us (8%)
  matrix products  32.1 us (6%)
  blocking collectives  29.7 us (6%)
  local copies, waits for them, and re-layouts  19 us (4%)
  between operations  14.6 us (3%)
  other arithmetic  13.1 us (3%)
    ppermute x16, waiting for transfers between devices, from_behind(): return lax.ppermute(value, axis, pairs)  99.5 us
    reduce_scatter x1, waiting for transfers between devices, shards(): part = lax.psum_scatter(part, 'y', scatter_dimension=0, tiled=True)[0]  56.8 us
    reduce_scatter x1, waiting for transfers between devices, shards(): lax.psum_scatter(weight_part, 'c', scatter_dimension=0, tiled=True)[0]  49.6 us
    all_gather x1, waiting for transfers between devices, shards(): lax.all_gather(mine, 'dp', axis=0, tiled=True)  40 us
    ppermute x16, starting transfers between devices, from_behind(): return lax.ppermute(value, axis, pairs)  39.7 us
    unnamed x8, waiting for transfers between devices  35.3 us
    reduce_scatter x1, waiting for transfers between devices, shards(): part = lax.psum_scatter(part, 'dp', scatter_dimension=0, tiled=True)[0]  27.4 us
    all_gather x1, waiting for transfers between devices, shards(): lax.all_gather(lax.all_gather(mine, 'dp', axis=0, tiled=True), 'c', axis=0)  22 us
  transfers between devices with their start and end apart: 23, of which 14 were waited for; matrix products, arithmetic and copies ran while one was open for 4% of the time, Pallas kernels for 0%

profile of v2, /device:TPU:1, one launch (start us, length us, event | category | flops | bytes accessed | tf_op | source)
XLA Modules:
  0.0 495.4 jit_solution(1466209624229195306)
XLA Ops:
  7.2 2.2 fusion.36
  9.5 40.0 %all-gather.7.cloned.1.call-done = bf16[1,2304,512]{2,1,0:T(8,128)(2,1)} async-done(((bf16[1,576,512]{2,1,0:T(8,128)(2,1)}), bf16[1,2304,512]{2,1,0:T(8,128)(2,1)}) %all-gather.7.cloned.1.call-update) | async-done | bytes 2359312 | tf_op jit(solution)/shard_map/all_gather | solution.py:103
  50.1 22.0 %all-gather.9.cloned.1.call-done = bf16[2,2304,512]{2,1,0:T(8,128)(2,1)} async-done(((bf16[1,2304,512]{2,1,0:T(8,128)(2,1)}), bf16[2,2304,512]{2,1,0:T(8,128)(2,1)}) %all-gather.9.cloned.1.call-update) | async-done | bytes 4718608 | tf_op jit(solution)/shard_map/all_gather | solution.py:103
  72.1 2.6 fusion.23
  74.7 0.4 copy-done.2
  75.2 0.8 fusion.20
  76.0 0.8 pad_maximum_fusion.1
  76.8 3.7 collective-permute-start
  80.5 3.6 collective-permute-start.1
  84.1 4.4 collective-permute-start.2
  88.5 3.6 collective-permute-start.3
  92.1 4.3 collective-permute-start.4
  96.4 2.1 fusion.9
  99.0 4.3 collective-permute-start.5
  103.4 1.1 constant_dynamic-update-slice_fusion.8
  104.4 2.5 collective-permute-start.6
  107.0 1.1 constant_dynamic-update-slice_fusion.7
  108.0 14.1 %collective-permute-done.2 = bf16[256,1024]{0,1:T(8,128)(2,1)} collective-permute-done((bf16[256,1024]{0,1:T(8,128)(2,1)}, bf16[256,1024]{0,1:T(8,128)(2,1)}, u32[]{:S(2)}, u32[]{:S(2)}) %collective-permute-start.2) | collective-permute-done | bytes 524320 | tf_op jit(solution)/shard_map/ppermute | solution.py:24
  122.2 2.1 collective-permute-start.7
  124.3 1.1 constant_dynamic-update-slice_fusion.6
  125.4 5.9 %collective-permute-done.3 = bf16[256,1024]{0,1:T(8,128)(2,1)} collective-permute-done((bf16[256,1024]{0,1:T(8,128)(2,1)}, bf16[256,1024]{0,1:T(8,128)(2,1)}, u32[]{:S(2)}, u32[]{:S(2)}) %collective-permute-start.3) | collective-permute-done | bytes 524320 | tf_op jit(solution)/shard_map/ppermute | solution.py:24
  131.2 1.1 constant_dynamic-update-slice_fusion.5
  132.3 1.1 constant_dynamic-update-slice_fusion.4
  133.5 4.8 collective-permute-done.7
  138.7 1.9 fusion.42
  140.6 1.3 exponential_reduce_fusion
  141.9 1.5 fusion.13
  143.4 2.4 multiply_reduce_fusion
  145.9 4.8 fusion.3
  150.7 3.8 fusion.43
  154.4 2.9 fusion
  157.4 0.8 copy-done
  158.2 3.7 fusion.39
  161.9 1.3 collective-permute-start.15
  163.2 1.3 collective-permute-start.14
  164.5 1.3 collective-permute-start.13
  165.8 1.3 collective-permute-start.12
  167.1 1.3 collective-permute-start.11
  168.4 27.4 %collective-permute-done.15 = bf16[256,1024]{0,1:T(8,128)(2,1)S(1)} collective-permute-done((bf16[256,1024]{0,1:T(8,128)(2,1)S(1)}, bf16[256,1024]{0,1:T(8,128)(2,1)S(1)}, u32[]{:S(2)}, u32[]{:S(2)}) %collective-permute-start.15) | collective-permute-done | bytes 524320 | tf_op jit(solution)/shard_map/ppermute | solution.py:24
  195.7 1.3 collective-permute-start.10
  197.0 22.5 %collective-permute-done.14 = bf16[256,1024]{0,1:T(8,128)(2,1)S(1)} collective-permute-done((bf16[256,1024]{0,1:T(8,128)(2,1)S(1)}, bf16[256,1024]{0,1:T(8,128)(2,1)S(1)}, u32[]{:S(2)}, u32[]{:S(2)}) %collective-permute-start.14) | collective-permute-done | bytes 524320 | tf_op jit(solution)/shard_map/ppermute | solution.py:24
  219.5 1.3 collective-permute-start.9
  220.8 2.1 collective-permute-start.8
  223.0 1.6 copy.69
  224.6 23.9 %collective-permute-done.9 = bf16[256,1024]{0,1:T(8,128)(2,1)} collective-permute-done((bf16[256,1024]{0,1:T(8,128)(2,1)}, bf16[256,1024]{0,1:T(8,128)(2,1)}, u32[]{:S(2)}, u32[]{:S(2)}) %collective-permute-start.9) | collective-permute-done | bytes 524320 | tf_op jit(solution)/shard_map/ppermute | solution.py:24
  248.5 0.9 collective-permute-done.8
  249.5 2.6 fusion.35
  252.0 4.5 convolution_bitcast_fusion
  256.6 49.6 %reduce-scatter.7.cloned.1.call-done = f32[1,4,4,8,72,128]{5,4,3,2,1,0:T(8,128)} async-done(((f32[2,4,4,8,72,128]{5,4,3,2,1,0:T(8,128)}), f32[1,4,4,8,72,128]{5,4,3,2,1,0:T(8,128)}) %reduce-scatter.7.cloned.1.call-update) | async-done | bytes 4718608 | tf_op jit(solution)/shard_map/reduce_scatter | solution.py:159
  306.3 56.8 %reduce-scatter.9.cloned.1.call-done = f32[1,4,8,72,128]{4,3,2,1,0:T(8,128)} async-done(((f32[4,4,8,72,128]{4,3,2,1,0:T(8,128)}), f32[1,4,8,72,128]{4,3,2,1,0:T(8,128)}) %reduce-scatter.9.cloned.1.call-update) | async-done | bytes 1179664 | tf_op jit(solution)/shard_map/reduce_scatter | solution.py:160
  363.1 27.4 %reduce-scatter.11.cloned.1.call-done = f32[1,8,72,128]{3,2,1,0:T(8,128)} async-done(((f32[4,8,72,128]{3,2,1,0:T(8,128)}), f32[1,8,72,128]{3,2,1,0:T(8,128)}) %reduce-scatter.11.cloned.1.call-update) | async-done | bytes 294928 | tf_op jit(solution)/shard_map/reduce_scatter | solution.py:161
  390.6 1.0 copy.72
  391.6 35.1 %reduce-scatter.13.cloned.1.call-done = f32[1,72,128]{2,1,0:T(8,128)} async-done(((f32[8,72,128]{2,1,0:T(8,128)}), f32[1,72,128]{2,1,0:T(8,128)}) %reduce-scatter.13.cloned.1.call-update) | async-done | bytes 36880
  426.8 0.8 convert_element_type.107
  427.5 18.2 %all_gather.24 = bf16[8,72,128]{2,1,0:T(8,128)(2,1)S(1)} all-gather(bf16[1,72,128]{2,1,0:T(8,128)(2,1)S(1)} %convert_element_type.107), channel_id=1, replica_groups=mesh['dp'=4,'z'=8,'y'=4,'c'=2] {'z'}, dimensions={0}, use_global_device_ids=true | all-gather | bytes 165888 | tf_op jit(solution)/shard_map/all_gather | solution.py:164
  445.8 11.4 %all_gather.25 = bf16[4,576,128]{2,1,0:T(8,128)(2,1)} all-gather(bf16[1,576,128]{2,1,0:T(8,128)(2,1)S(1)} %bitcast.132), channel_id=1, replica_groups=mesh['dp'=4,'z'=8,'y'=4,'c'=2] {'y'}, dimensions={0}, use_global_device_ids=true | all-gather | bytes 737280 | tf_op jit(solution)/shard_map/all_gather | solution.py:165
  457.2 3.7 convolution_convert_fusion
  461.0 1.0 copy.73
  462.0 2.5 fusion.11
  464.5 3.5 fusion.6
  468.0 16.4 %all-gather.11.cloned.1.call-done = bf16[8,576,128]{2,1,0:T(8,128)(2,1)} async-done(((bf16[4,576,128]{2,1,0:T(8,128)(2,1)}), bf16[8,576,128]{2,1,0:T(8,128)(2,1)}) %all-gather.11.cloned.1.call-update) | async-done | bytes 1179664 | tf_op jit(solution)/shard_map/all_gather | solution.py:166
  484.4 2.2 copy.71
  486.6 0.9 reshape.172
  487.5 1.1 fusion.41
  (64 shorter events, 1.8 us)
Async XLA Ops:
  7.2 42.4 %copy-start.12 = (s32[1,16]{1,0:T(1,128)S(1)}, s32[1,16]{1,0:T(1,128)}, u32[]{:S(2)}) copy-start(s32[1,16]{1,0:T(1,128)} %param.10) | copy-start | bytes 196
  7.2 64.9 %copy-start.7 = (bf16[1,256,2304]{2,1,0:T(8,128)(2,1)S(1)}, bf16[1,256,2304]{2,1,0:T(8,128)(2,1)}, u32[]{:S(2)}) copy-start(bf16[1,256,2304]{2,1,0:T(8,128)(2,1)} %param.6) | copy-start | bytes 3538948
  7.2 42.3 %all-gather.7.cloned.1.call-start = ((), (), s32[]{:S(2)}) async-start(), calls=%async_computation.7 | async-start | bytes 2949120 | tf_op jit(solution)/shard_map/all_gather | solution.py:103
  9.4 62.7 %all-gather.9.cloned.1.call-start = ((), (), s32[]{:S(2)}) async-start(), calls=%async_computation.8 | async-start | bytes 7077888 | tf_op jit(solution)/shard_map/all_gather | solution.py:103
  49.5 256.7 %reduce-scatter.7.cloned.1.call-start = ((), (), s32[]{:S(2)}) async-start(), calls=%async_computation.4 | async-start | bytes 14155776 | tf_op jit(solution)/shard_map/reduce_scatter | solution.py:159
  72.1 3.0 copy-start.2
  75.2 23.4 %copy-start.9 = (bf16[1,256,1024]{2,1,0:T(8,128)(2,1)S(1)}, bf16[1,256,1024]{2,1,0:T(8,128)(2,1)}, u32[]{:S(2)}) copy-start(bf16[1,256,1024]{2,1,0:T(8,128)(2,1)} %param.11) | copy-start | bytes 1572868
  75.2 23.7 %copy-start.10 = (bf16[1,256,1024]{2,1,0:T(8,128)(2,1)S(1)}, bf16[1,256,1024]{2,1,0:T(8,128)(2,1)}, u32[]{:S(2)}) copy-start(bf16[1,256,1024]{2,1,0:T(8,128)(2,1)} %param.7) | copy-start | bytes 1572868
  76.8 22.2 %collective-permute-start = (bf16[256,1024]{0,1:T(8,128)(2,1)}, bf16[256,1024]{0,1:T(8,128)(2,1)}, u32[]{:S(2)}, u32[]{:S(2)}) collective-permute-start(bf16[256,1024]{0,1:T(8,128)(2,1)} %pad_maximum_fusion.1), channel_id=1, source_target_pairs={{0,8},{1,9},{2,10},{3,11},{4,12},{5,13},{6,14},{7,15},{8,16},{9,17... | collective-permute-start | bytes 1572872 | tf_op jit(solution)/shard_map/ppermute | solution.py:24
  80.5 23.9 %collective-permute-start.1 = (bf16[256,1024]{0,1:T(8,128)(2,1)}, bf16[256,1024]{0,1:T(8,128)(2,1)}, u32[]{:S(2)}, u32[]{:S(2)}) collective-permute-start(bf16[256,1024]{0,1:T(8,128)(2,1)} %pad_maximum_fusion.1), channel_id=1, source_target_pairs={{0,7},{1,8},{2,9},{3,10},{4,11},{5,12},{6,13},{7,14},{8,15},{9,16}... | collective-permute-start | bytes 1572872 | tf_op jit(solution)/shard_map/ppermute | solution.py:24
  84.1 38.1 %collective-permute-start.2 = (bf16[256,1024]{0,1:T(8,128)(2,1)}, bf16[256,1024]{0,1:T(8,128)(2,1)}, u32[]{:S(2)}, u32[]{:S(2)}) collective-permute-start(bf16[256,1024]{0,1:T(8,128)(2,1)} %pad_maximum_fusion.1), channel_id=1, source_target_pairs={{0,6},{1,7},{2,8},{3,9},{4,10},{5,11},{6,12},{7,13},{8,14},{9,15},... | collective-permute-start | bytes 1572872 | tf_op jit(solution)/shard_map/ppermute | solution.py:24
  88.5 42.7 %collective-permute-start.3 = (bf16[256,1024]{0,1:T(8,128)(2,1)}, bf16[256,1024]{0,1:T(8,128)(2,1)}, u32[]{:S(2)}, u32[]{:S(2)}) collective-permute-start(bf16[256,1024]{0,1:T(8,128)(2,1)} %pad_maximum_fusion.1), channel_id=1, source_target_pairs={{0,5},{1,6},{2,7},{3,8},{4,9},{5,10},{6,11},{7,12},{8,13},{9,14},{... | collective-permute-start | bytes 1572872 | tf_op jit(solution)/shard_map/ppermute | solution.py:24
  92.1 40.2 %collective-permute-start.4 = (bf16[256,1024]{0,1:T(8,128)(2,1)}, bf16[256,1024]{0,1:T(8,128)(2,1)}, u32[]{:S(2)}, u32[]{:S(2)}) collective-permute-start(bf16[256,1024]{0,1:T(8,128)(2,1)} %pad_maximum_fusion.1), channel_id=1, source_target_pairs={{0,4},{1,5},{2,6},{3,7},{4,8},{5,9},{6,10},{7,11},{8,12},{9,13},{1... | collective-permute-start | bytes 1572872 | tf_op jit(solution)/shard_map/ppermute | solution.py:24
  99.0 39.6 %copy-start.5 = (bf16[1,256,1024]{1,2,0:T(8,128)(2,1)}, bf16[1,256,1024]{1,2,0:T(8,128)(2,1)S(1)}, u32[]{:S(2)}) copy-start(bf16[1,256,1024]{1,2,0:T(8,128)(2,1)S(1)} %copy.93) | copy-start | bytes 1572868
  99.0 34.3 %collective-permute-start.5 = (bf16[256,1024]{0,1:T(8,128)(2,1)}, bf16[256,1024]{0,1:T(8,128)(2,1)S(1)}, u32[]{:S(2)}, u32[]{:S(2)}) collective-permute-start(bf16[256,1024]{0,1:T(8,128)(2,1)} %pad_maximum_fusion.1), channel_id=1, source_target_pairs={{0,3},{1,4},{2,5},{3,6},{4,7},{5,8},{6,9},{7,10},{8,11},{9,12},{10... | collective-permute-start | bytes 1572872 | tf_op jit(solution)/shard_map/ppermute | solution.py:24
  104.4 29.0 %collective-permute-start.6 = (bf16[256,1024]{0,1:T(8,128)(2,1)}, bf16[256,1024]{0,1:T(8,128)(2,1)S(1)}, u32[]{:S(2)}, u32[]{:S(2)}) collective-permute-start(bf16[256,1024]{0,1:T(8,128)(2,1)} %pad_maximum_fusion.1), channel_id=1, source_target_pairs={{0,2},{1,3},{2,4},{3,5},{4,6},{5,7},{6,8},{7,9},{8,10},{9,11},{10,... | collective-permute-start | bytes 1572872 | tf_op jit(solution)/shard_map/ppermute | solution.py:24
  122.2 16.1 %collective-permute-start.7 = (bf16[256,1024]{0,1:T(8,128)(2,1)}, bf16[256,1024]{0,1:T(8,128)(2,1)S(1)}, u32[]{:S(2)}, u32[]{:S(2)}) collective-permute-start(bf16[256,1024]{0,1:T(8,128)(2,1)} %pad_maximum_fusion.1), channel_id=1, source_target_pairs={{0,1},{1,2},{2,3},{3,4},{4,5},{5,6},{6,7},{7,8},{8,9},{9,10},{10,1... | collective-permute-start | bytes 1572872 | tf_op jit(solution)/shard_map/ppermute | solution.py:24
  138.7 2.0 copy-start.3
  143.4 11.0 %copy-start.1 = (f32[2,2304,256,1]{1,2,3,0:T(8,128)}, f32[2,2304,256,1]{1,2,3,0:T(8,128)S(1)}, u32[]{:S(2)}) copy-start(f32[2,2304,256,1]{1,2,3,0:T(8,128)S(1)} %fusion.13) | copy-start | bytes 14155780
  145.9 4.8 copy-start.6
  154.4 3.7 copy-start
  161.9 33.9 %collective-permute-start.15 = (bf16[256,1024]{0,1:T(8,128)(2,1)S(1)}, bf16[256,1024]{0,1:T(8,128)(2,1)S(1)}, u32[]{:S(2)}, u32[]{:S(2)}) collective-permute-start(bf16[256,1024]{0,1:T(8,128)(2,1)S(1)} %get-tuple-element.26), channel_id=1, source_target_pairs={{8,0},{9,1},{10,2},{11,3},{12,4},{13,5},{14,6},{15,7},{16,8},{17,9... | collective-permute-start | bytes 1572872 | tf_op jit(solution)/shard_map/ppermute | solution.py:24
  163.2 56.3 %collective-permute-start.14 = (bf16[256,1024]{0,1:T(8,128)(2,1)S(1)}, bf16[256,1024]{0,1:T(8,128)(2,1)S(1)}, u32[]{:S(2)}, u32[]{:S(2)}) collective-permute-start(bf16[256,1024]{0,1:T(8,128)(2,1)S(1)} %get-tuple-element.27), channel_id=1, source_target_pairs={{7,0},{8,1},{9,2},{10,3},{11,4},{12,5},{13,6},{14,7},{15,8},{16,9}... | collective-permute-start | bytes 1572872 | tf_op jit(solution)/shard_map/ppermute | solution.py:24
  164.5 56.3 %collective-permute-start.13 = (bf16[256,1024]{0,1:T(8,128)(2,1)S(1)}, bf16[256,1024]{0,1:T(8,128)(2,1)S(1)}, u32[]{:S(2)}, u32[]{:S(2)}) collective-permute-start(bf16[256,1024]{0,1:T(8,128)(2,1)S(1)} %get-tuple-element.28), channel_id=1, source_target_pairs={{6,0},{7,1},{8,2},{9,3},{10,4},{11,5},{12,6},{13,7},{14,8},{15,9},... | collective-permute-start | bytes 1572872 | tf_op jit(solution)/shard_map/ppermute | solution.py:24
  165.8 58.8 %collective-permute-start.12 = (bf16[256,1024]{0,1:T(8,128)(2,1)}, bf16[256,1024]{0,1:T(8,128)(2,1)S(1)}, u32[]{:S(2)}, u32[]{:S(2)}) collective-permute-start(bf16[256,1024]{0,1:T(8,128)(2,1)} %get-tuple-element.29), channel_id=1, source_target_pairs={{5,0},{6,1},{7,2},{8,3},{9,4},{10,5},{11,6},{12,7},{13,8},{14,9},{... | collective-permute-start | bytes 1572872 | tf_op jit(solution)/shard_map/ppermute | solution.py:24
  167.1 57.5 %collective-permute-start.11 = (bf16[256,1024]{0,1:T(8,128)(2,1)}, bf16[256,1024]{0,1:T(8,128)(2,1)}, u32[]{:S(2)}, u32[]{:S(2)}) collective-permute-start(bf16[256,1024]{0,1:T(8,128)(2,1)} %get-tuple-element.30), channel_id=1, source_target_pairs={{4,0},{5,1},{6,2},{7,3},{8,4},{9,5},{10,6},{11,7},{12,8},{13,9},{1... | collective-permute-start | bytes 1572872 | tf_op jit(solution)/shard_map/ppermute | solution.py:24
  195.7 28.8 %collective-permute-start.10 = (bf16[256,1024]{0,1:T(8,128)(2,1)}, bf16[256,1024]{0,1:T(8,128)(2,1)}, u32[]{:S(2)}, u32[]{:S(2)}) collective-permute-start(bf16[256,1024]{0,1:T(8,128)(2,1)} %get-tuple-element.31), channel_id=1, source_target_pairs={{3,0},{4,1},{5,2},{6,3},{7,4},{8,5},{9,6},{10,7},{11,8},{12,9},{13... | collective-permute-start | bytes 1572872 | tf_op jit(solution)/shard_map/ppermute | solution.py:24
  219.5 29.0 %collective-permute-start.9 = (bf16[256,1024]{0,1:T(8,128)(2,1)}, bf16[256,1024]{0,1:T(8,128)(2,1)}, u32[]{:S(2)}, u32[]{:S(2)}) collective-permute-start(bf16[256,1024]{0,1:T(8,128)(2,1)} %get-tuple-element.32), channel_id=1, source_target_pairs={{2,0},{3,1},{4,2},{5,3},{6,4},{7,5},{8,6},{9,7},{10,8},{11,9},{12,... | collective-permute-start | bytes 1572872 | tf_op jit(solution)/shard_map/ppermute | solution.py:24
  220.8 28.6 %collective-permute-start.8 = (bf16[256,1024]{0,1:T(8,128)(2,1)}, bf16[256,1024]{0,1:T(8,128)(2,1)}, u32[]{:S(2)}, u32[]{:S(2)}) collective-permute-start(bf16[256,1024]{0,1:T(8,128)(2,1)} %get-tuple-element.25), channel_id=1, source_target_pairs={{1,0},{2,1},{3,2},{4,3},{5,4},{6,5},{7,6},{8,7},{9,8},{10,9},{11,1... | collective-permute-start | bytes 1572872 | tf_op jit(solution)/shard_map/ppermute | solution.py:24
  224.6 24.0 %copy-start.8 = (bf16[256,1024]{0,1:T(8,128)(2,1)}, bf16[256,1024]{0,1:T(8,128)(2,1)S(1)}, u32[]{:S(2)}) copy-start(bf16[256,1024]{0,1:T(8,128)(2,1)S(1)} %collective-permute-done.12) | copy-start | bytes 1572868
  256.5 134.1 %copy-start.11 = (bf16[2,256,2,256]{3,1,2,0:T(8,128)(2,1)S(1)}, bf16[2,256,2,256]{3,1,2,0:T(8,128)(2,1)}, u32[]{:S(2)}) copy-start(bf16[2,256,2,256]{3,1,2,0:T(8,128)(2,1)} %get-tuple-element.40) | copy-start | bytes 1572868
  256.5 200.7 %copy-start.4 = (bf16[2304,512]{0,1:T(8,128)(2,1)S(1)}, bf16[2304,512]{0,1:T(8,128)(2,1)}, u32[]{:S(2)}) copy-start(bf16[2304,512]{0,1:T(8,128)(2,1)} %copy-done.3) | copy-start | bytes 7077892
  256.6 106.5 %reduce-scatter.9.cloned.1.call-start = ((), (), s32[]{:S(2)}) async-start(), calls=%async_computation.5 | async-start | bytes 5898240 | tf_op jit(solution)/shard_map/reduce_scatter | solution.py:160
  306.2 84.3 %reduce-scatter.11.cloned.1.call-start = ((), (), s32[]{:S(2)}) async-start(), calls=%async_computation.6 | async-start | bytes 1474560 | tf_op jit(solution)/shard_map/reduce_scatter | solution.py:161
  363.1 63.7 %reduce-scatter.13.cloned.1.call-start = ((), (), s32[]{:S(2)}) async-start(), calls=%async_computation.10 | async-start | bytes 331776
  390.6 93.8 %all-gather.11.cloned.1.call-start = ((), (), s32[]{:S(2)}) async-start(), calls=%async_computation.9 | async-start | bytes 1769472 | tf_op jit(solution)/shard_map/all_gather | solution.py:166
Sparse Core Ops, SparseCore 0:
  10.4 39.0 all-gather.6
  51.3 20.7 all-gather.8
  256.7 49.4 reduce-scatter.6
  308.6 54.3 reduce-scatter.8
  365.5 25.0 reduce-scatter.10
  392.9 33.8 reduce-scatter.12
  457.4 27.0 all-gather.10
